TPU v7x, 256 devices: a whole 4x4x8 slice. The times are simulated.
256 devices in a mesh: tiles: 64 (over z, x, core), views: 4 (over y).
Axes of the slice: x: 4, y: 4, z: 8, core: 2. Of those that a mesh axis runs over, the one named last changes fastest.
Arguments:
- gaussians: float32 [59, 131072], P(None, 'tiles')
- moment_one: float32 [59, 131072], P(None, 'tiles'), may hold values from -3 to 3
- moment_two: float32 [59, 131072], P(None, 'tiles'), may hold values from 0.01 to 1
- learn_rates: float32 [59], replicated, may hold values from 0.002 to 0.05
- cameras: float32 [16, 12], replicated, as said below
- camera_ids: int32 [4], P('views'), may hold values from 0 to 15
- list_owner: int32 [4, 64, 1024, 1], P('views', 'tiles'), may hold values from 0 to 63; in each aligned block of 1024 rows (0 to 1023, 1024 to 2047, ..., all dimensions but the last counted through in order) at most 32 rows name the same one
- list_index: int32 [4, 64, 1024], P('views', 'tiles'), may hold values from 0 to 2047
- list_length: int32 [4, 64], P('views', 'tiles'), may hold values from 1 to 1024, 32768 in all within a row
- targets: bfloat16 [4, 64, 3, 1024], P('views', 'tiles'), may hold values from 0 to 1
- background: float32 [3], replicated, may hold values from 0.1 to 0.9
Outputs:
- rendered: bfloat16 [4, 64, 3, 1024], P('views', 'tiles')
- new_gaussians: float32 [59, 131072], P(None, 'tiles')
- new_moment_one: float32 [59, 131072], P(None, 'tiles')
- new_moment_two: float32 [59, 131072], P(None, 'tiles')
Inputs may be any that keep to these rules, and one draw needn't show every extreme that they name: `list_owner`: in the list of one device (one camera slot, one tile) no owner is named by more than 32 entries, and some device's list reaches this bound. `cameras`: rotations are proper, and every Gaussian lies in front of every camera.
All inputs are finite; a program needn't handle non-finite values. No bound on the sum of `list_length` on one device may be relied on, other than what follows from the above.
Results may differ from a plain program's by a relative error of at most 0.001.
Values sent between devices are 32-bit elements; how exact they have to be, the bound alone decides.
No kernel may reach another device: no remote copies, remote signals or barrier semaphores. Data moves between devices by JAX's collectives and lax.ppermute only.
A program may use at most 192 MiB of HBM per device.

v0:
```python
from functools import partial
import jax
import jax.numpy as jnp
from jax import lax
from jax.sharding import PartitionSpec as P

TILE_SIDE = 32
PIXELS = 1024
TILE_ROWS = 8
LIST = 1024
BLOCK = 128
focal_length = 400.0
precise = lax.Precision.HIGHEST
decay_one = 0.9
decay_two = 0.999
adam_epsilon = 1e-08


def sh_basis(direction):
    dir_x, dir_y, dir_z = (direction[0], direction[1], direction[2])
    sq_x, sq_y, sq_z = (dir_x * dir_x, dir_y * dir_y, dir_z * dir_z)
    terms = [
        0.28209479177387814 * jnp.ones_like(dir_x),
        -0.4886025119029199 * dir_y,
        0.4886025119029199 * dir_z,
        -0.4886025119029199 * dir_x,
        1.0925484305920792 * dir_x * dir_y,
        -1.0925484305920792 * dir_y * dir_z,
        0.31539156525252005 * (2.0 * sq_z - sq_x - sq_y),
        -1.0925484305920792 * dir_x * dir_z,
        0.5462742152960396 * (sq_x - sq_y),
        -0.5900435899266435 * dir_y * (3.0 * sq_x - sq_y),
        2.890611442640554 * dir_x * dir_y * dir_z,
        -0.4570457994644658 * dir_y * (4.0 * sq_z - sq_x - sq_y),
        0.3731763325901154 * dir_z * (2.0 * sq_z - 3.0 * sq_x - 3.0 * sq_y),
        -0.4570457994644658 * dir_x * (4.0 * sq_z - sq_x - sq_y),
        1.445305721320277 * dir_z * (sq_x - sq_y),
        -0.5900435899266435 * dir_x * (sq_x - 3.0 * sq_y),
    ]
    return jnp.stack(terms)


def quat_rotation(quat):
    length = jnp.sqrt(jnp.sum(quat * quat, axis=0))
    quat_w, quat_x, quat_y, quat_z = (
        quat[0] / length,
        quat[1] / length,
        quat[2] / length,
        quat[3] / length,
    )
    rows = [
        [
            1.0 - 2.0 * (quat_y * quat_y + quat_z * quat_z),
            2.0 * (quat_x * quat_y - quat_w * quat_z),
            2.0 * (quat_x * quat_z + quat_w * quat_y),
        ],
        [
            2.0 * (quat_x * quat_y + quat_w * quat_z),
            1.0 - 2.0 * (quat_x * quat_x + quat_z * quat_z),
            2.0 * (quat_y * quat_z - quat_w * quat_x),
        ],
        [
            2.0 * (quat_x * quat_z - quat_w * quat_y),
            2.0 * (quat_y * quat_z + quat_w * quat_x),
            1.0 - 2.0 * (quat_x * quat_x + quat_y * quat_y),
        ],
    ]
    return jnp.stack([jnp.stack(entries) for entries in rows])


def project(params, camera, center_x, center_y):
    means = params[0:3]
    rotate = camera[0:9].reshape(3, 3)
    shift = camera[9:12]
    view_pos = jnp.dot(rotate, means, precision=precise) + shift[:, None]
    inv_depth = 1.0 / view_pos[2]
    image_x = focal_length * view_pos[0] * inv_depth + center_x
    image_y = focal_length * view_pos[1] * inv_depth + center_y
    scales = jnp.exp(params[3:6])
    local_axes = quat_rotation(params[6:10]) * scales[None, :, :]
    world_axes = jnp.einsum("ik,kjg->ijg", rotate, local_axes, precision=precise)
    proj_x = (
        focal_length * inv_depth * world_axes[0]
        - focal_length * view_pos[0] * inv_depth * inv_depth * world_axes[2]
    )
    proj_y = (
        focal_length * inv_depth * world_axes[1]
        - focal_length * view_pos[1] * inv_depth * inv_depth * world_axes[2]
    )
    cov_xx = jnp.sum(proj_x * proj_x, axis=0) + 0.3
    cov_xy = jnp.sum(proj_x * proj_y, axis=0)
    cov_yy = jnp.sum(proj_y * proj_y, axis=0) + 0.3
    determ = cov_xx * cov_yy - cov_xy * cov_xy
    opacity = 0.99 * jax.nn.sigmoid(params[10])
    center = -jnp.dot(rotate.T, shift, precision=precise)
    offset = means - center[:, None]
    direction = offset / jnp.sqrt(jnp.sum(offset * offset, axis=0))
    basis = sh_basis(direction)
    coeffs = params[11:59].reshape(16, 3, -1)
    colors = 0.5 + jnp.sum(basis[:, None, :] * coeffs, axis=0)
    head = jnp.stack(
        [image_x, image_y, cov_yy / determ, -cov_xy / determ, cov_xx / determ, opacity]
    )
    return jnp.concatenate([head, colors], axis=0)


def pixel_grid(tile, tile_cols):
    offsets = jnp.arange(PIXELS)
    pixel_x = (tile % tile_cols * TILE_SIDE + offsets % TILE_SIDE).astype(jnp.float32) + 0.5
    pixel_y = (tile // tile_cols * TILE_SIDE + offsets // TILE_SIDE).astype(jnp.float32) + 0.5
    return (pixel_x, pixel_y)


def block_terms(entry, count, pixel_x, pixel_y, index):
    start = index * BLOCK
    piece = lax.dynamic_slice_in_dim(entry, start, BLOCK, 1)
    live = (start + jnp.arange(BLOCK) < count)[None, :]
    delta_x = pixel_x[:, None] - piece[0][None, :]
    delta_y = pixel_y[:, None] - piece[1][None, :]
    power = -0.5 * (
        piece[2] * delta_x * delta_x
        + 2.0 * piece[3] * delta_x * delta_y
        + piece[4] * delta_y * delta_y
    )
    falloff = jnp.exp(power)
    alpha = jnp.where(live, piece[5][None, :] * falloff, 0.0)
    log_keep = jnp.log1p(-alpha)
    return (start, piece, live, delta_x, delta_y, falloff, alpha, log_keep)


def tile_pass(entry, count, pixel_x, pixel_y, target, background):
    blocks = (count + BLOCK - 1) // BLOCK

    def forward(index, carry):
        color, log_total = carry
        start, piece, live, delta_x, delta_y, falloff, alpha, log_keep = block_terms(
            entry, count, pixel_x, pixel_y, index
        )
        weight = jnp.exp(log_total[:, None] + jnp.cumsum(log_keep, axis=1) - log_keep) * alpha
        color = color + lax.dot_general(
            piece[6:9], weight, (((1,), (1,)), ((), ())), precision=precise
        )
        return (color, log_total + jnp.sum(log_keep, axis=1))

    zeros_pix = jnp.zeros((PIXELS,), jnp.float32)
    color, log_total = lax.fori_loop(
        0, blocks, forward, (jnp.zeros((3, PIXELS), jnp.float32), zeros_pix)
    )
    image = color + jnp.exp(log_total)[None, :] * background[:, None]
    resid = image - target
    dot_total = jnp.sum(image * resid, axis=0)

    def backward(index, carry):
        grads, log_before, prefix = carry
        start, piece, live, delta_x, delta_y, falloff, alpha, log_keep = block_terms(
            entry, count, pixel_x, pixel_y, index
        )
        trans = jnp.exp(log_before[:, None] + jnp.cumsum(log_keep, axis=1) - log_keep)
        weight = trans * alpha
        along = lax.dot_general(resid, piece[6:9], (((0,), (0,)), ((), ())), precision=precise)
        running = prefix[:, None] + jnp.cumsum(weight * along, axis=1)
        d_alpha = jnp.where(
            live, trans * along - (dot_total[:, None] - running) / (1.0 - alpha), 0.0
        )
        d_power = d_alpha * alpha
        sum_x = jnp.sum(d_power * delta_x, axis=0)
        sum_y = jnp.sum(d_power * delta_y, axis=0)
        head = jnp.stack(
            [
                piece[2] * sum_x + piece[3] * sum_y,
                piece[3] * sum_x + piece[4] * sum_y,
                -0.5 * jnp.sum(d_power * delta_x * delta_x, axis=0),
                -jnp.sum(d_power * delta_x * delta_y, axis=0),
                -0.5 * jnp.sum(d_power * delta_y * delta_y, axis=0),
                jnp.sum(d_alpha * falloff, axis=0),
            ]
        )
        color_grad = jnp.dot(resid, weight, precision=precise)
        block_grad = jnp.concatenate([head, color_grad], axis=0)
        grads = lax.dynamic_update_slice_in_dim(grads, block_grad, start, 1)
        return (grads, log_before + jnp.sum(log_keep, axis=1), running[:, -1])

    start_grads = jnp.zeros((9, LIST), jnp.float32)
    grads, ignored, unused = lax.fori_loop(0, blocks, backward, (start_grads, zeros_pix, zeros_pix))
    return (image, grads)


def adam_step(values, first, second, grad, rates):
    first_new = decay_one * first + (1.0 - decay_one) * grad
    second_new = decay_two * second + (1.0 - decay_two) * grad * grad
    return (
        values - rates[:, None] * first_new / (jnp.sqrt(second_new) + adam_epsilon),
        first_new,
        second_new,
    )


def body(
    gaussians,
    moment_one,
    moment_two,
    learn_rates,
    cameras,
    camera_ids,
    list_owner,
    list_index,
    list_length,
    targets,
    background,
):
    peers = lax.axis_size("tiles")
    tiles_here = list_index.shape[1]
    entries = tiles_here * LIST
    owned = gaussians.shape[1]
    capacity = 2 * entries // peers
    tile_cols = tiles_here * peers // TILE_ROWS
    center_x = 0.5 * TILE_SIDE * tile_cols
    center_y = 0.5 * TILE_SIDE * TILE_ROWS
    camera = cameras[camera_ids[0]]
    attrs, pullback = jax.vjp(
        partial(project, camera=camera, center_x=center_x, center_y=center_y), gaussians
    )
    owner_flat = list_owner.reshape(-1)
    index_flat = list_index.reshape(-1)
    order = jnp.argsort(owner_flat, stable=True)
    sorted_owner = owner_flat[order]
    one_hot = (sorted_owner[:, None] == jnp.arange(peers)[None, :]).astype(jnp.int32)
    counts = jnp.sum(one_hot, axis=0)
    starts = jnp.cumsum(counts) - counts
    rank = jnp.arange(entries) - jnp.sum(one_hot * starts[None, :], axis=1)
    slot = sorted_owner * capacity + rank
    position = jnp.zeros((entries,), jnp.int32).at[order].set(slot)
    asked_for = (
        jnp.zeros((peers * capacity,), jnp.int32)
        .at[slot]
        .set(index_flat[order])
        .reshape(peers, capacity)
    )
    asked = lax.all_to_all(asked_for, "tiles", split_axis=0, concat_axis=0, tiled=True)
    served = jnp.take(attrs, asked, axis=1)
    returned = lax.all_to_all(served, "tiles", split_axis=1, concat_axis=1, tiled=True)
    entry_attrs = returned.reshape(9, peers * capacity)[:, position].reshape(9, tiles_here, LIST)
    first_tile = lax.axis_index("tiles") * tiles_here

    def render(item):
        local_tile, entry, count, target = item
        pixel_x, pixel_y = pixel_grid(first_tile + local_tile, tile_cols)
        return tile_pass(entry, count, pixel_x, pixel_y, target.astype(jnp.float32), background)

    images, tile_grads = lax.map(
        render,
        (jnp.arange(tiles_here), jnp.moveaxis(entry_attrs, 1, 0), list_length[0], targets[0]),
    )
    flat_grads = jnp.moveaxis(tile_grads, 0, 1).reshape(9, entries)
    global_ids = owner_flat * owned + index_flat
    dense = jnp.zeros((9, peers * owned), jnp.float32).at[:, global_ids].add(flat_grads)
    attr_grad = lax.psum_scatter(dense, "tiles", scatter_dimension=1, tiled=True)
    param_grad = pullback(attr_grad)[0]
    total = lax.psum(param_grad, "views")
    new_values, first_new, second_new = adam_step(
        gaussians, moment_one, moment_two, total, learn_rates
    )
    return (images[None].astype(jnp.bfloat16), new_values, first_new, second_new)


def solution(mesh):
    return jax.shard_map(
        body,
        mesh=mesh,
        in_specs=(
            P(None, "tiles"),
            P(None, "tiles"),
            P(None, "tiles"),
            P(),
            P(),
            P("views"),
            P("views", "tiles", None, None),
            P("views", "tiles", None),
            P("views", "tiles"),
            P("views", "tiles", None, None),
            P(),
        ),
        out_specs=(
            P("views", "tiles", None, None),
            P(None, "tiles"),
            P(None, "tiles"),
            P(None, "tiles"),
        ),
        check_vma=False,
    )
```

profile of v0, /device:TPU:2, one launch (start us, length us, event | category | flops | bytes accessed | tf_op | source)
XLA Modules:
  0.0 475.0 jit_solution(15722905798426778904)
XLA Ops:
  7.2 5.1 %sort.17 = (s32[1024]{0:T(1024)}, s32[1024]{0:T(1024)S(1)}) sort(s32[1024]{0:T(1024)} %bitcast.355, s32[1024]{0:T(1024)S(1)} %iota.30), dimensions={0}, to_apply=%region_0.0 | sort | flops 10240 | bytes 16384 | tf_op jit(solution)/shard_map/jit(argsort)/sort | solution.py:225
  12.3 5.7 %gather_fusion = s32[1024]{0:T(1024)S(1)} fusion(s32[1024]{0:T(1024)} %bitcast.356, s32[1024]{0:T(1024)S(1)} %get-tuple-element.458), kind=kCustom, calls=%fused_computation | custom fusion | bytes 12288 | tf_op jit(solution)/shard_map/gather | solution.py:226
  18.0 5.7 %gather_fusion.1 = s32[1024]{0:T(1024)S(1)} fusion(s32[1024]{0:T(1024)} %bitcast.357, s32[1024]{0:T(1024)S(1)} %get-tuple-element.458), kind=kCustom, calls=%fused_computation.1 | custom fusion | bytes 12288 | tf_op jit(solution)/shard_map/gather | solution.py:236
  24.3 4.3 scatter_custom_fusion
  29.3 12.0 %all-to-all-start = ((s32[64,1,32]{2,1,0:T(1,128)}), s32[64,1,32]{2,1,0:T(1,128)S(1)}, u32[]{:S(2)}, u32[]{:S(2)}) async-start(s32[64,1,32]{2,1,0:T(1,128)} %bitcast.7), calls=%async_computation | async-start | bytes 65536 | tf_op jit(solution)/shard_map/all_to_all | solution.py:239
  42.8 0.9 multiply_reduce_fusion.9
  43.8 1.1 slice.164
  45.2 0.9 multiply_reduce_fusion.5
  46.2 1.0 convolution_add_fusion.2
  47.3 1.0 broadcast_divide_fusion
  48.3 1.7 broadcast_multiply_fusion.10
  50.1 1.0 subtract_multiply_fusion.21
  52.3 4.4 sort.18
  58.6 4.3 scatter_custom_fusion.1
  63.0 5.5 %gather_fusion.2 = f32[2048,9]{1,0:T(8,128)S(1)} fusion(f32[9,2048]{0,1:T(8,128)S(1)} %copy.61, s32[2048]{0:T(1024)S(1)} %broadcast_clamp_fusion), kind=kCustom, calls=%fused_computation.2 | custom fusion | bytes 155648 | tf_op jit(solution)/shard_map/jit(_take)/gather | solution.py:240
  69.9 10.3 %all-to-all-start.1 = ((f32[64,1,288]{2,1,0:T(1,128)}), f32[64,1,288]{2,1,0:T(1,128)S(1)}, u32[]{:S(2)}, u32[]{:S(2)}) async-start(f32[64,1,288]{2,1,0:T(1,128)} %reshape.822), calls=%async_computation.1 | async-start | bytes 196608 | tf_op jit(solution)/shard_map/all_to_all | solution.py:241
  80.3 9.3 %all-to-all-done.1 = f32[64,1,288]{2,1,0:T(1,128)S(1)} async-done(((f32[64,1,288]{2,1,0:T(1,128)}), f32[64,1,288]{2,1,0:T(1,128)S(1)}, u32[]{:S(2)}, u32[]{:S(2)}) %all-to-all-start.1) | async-done | bytes 73760 | tf_op jit(solution)/shard_map/all_to_all | solution.py:241
  91.6 2.8 gather_fusion.3
  94.6 22.7 %while.40 = (s32[]{:T(128)}, f32[3,1024]{1,0:T(4,128)S(1)}, f32[1024]{0:T(1024)S(1)}, s32[]{:T(128)}, f32[9,1024]{1,0:T(8,128)S(1)}, /*index=5*/s32[]{:T(128)}, ...) while((s32[]{:T(128)}, f32[3,1024]{1,0:T(4,128)S(1)}, ...), condition=%wide.region_15.16_spmd.clone, body=%wide.region_12.15_spmd.clone.sunk | while | flops 25580940 | bytes 2186327 | solution.py:146
  96.9 1.0 convolution_add_fusion.4
  99.6 1.0 convolution_add_fusion.4
  102.4 1.0 convolution_add_fusion.4
  105.2 1.0 convolution_add_fusion.4
  108.0 1.0 convolution_add_fusion.4
  110.7 1.0 convolution_add_fusion.4
  113.5 1.0 convolution_add_fusion.4
  116.3 1.0 convolution_add_fusion.4
  117.3 1.4 multiply_reduce_fusion.10
  118.7 65.1 %while.41 = (s32[]{:T(128)}, f32[9,1024]{1,0:T(8,128)S(1)}, f32[1024]{0:T(1024)S(1)}, f32[1024]{0:T(1024)S(1)}, s32[]{:T(128)}, /*index=5*/f32[9,1024]{1,0:T(8,1...) while((s32[]{:T(128)}, f32[9,1024]{1,0:T(8,128)S(1)}, ...), condition=%wide.region_27.28_spmd.clone, body=%wide.region_17.27_spmd.clone.sunk | while | flops 55855884 | bytes 9094147 | solution.py:184
  120.5 1.8 convolution_bitcast_fusion.4
  122.3 2.0 fusion.212
  124.7 0.9 fusion.213
  125.6 0.9 fusion.214
  128.6 1.8 convolution_bitcast_fusion.4
  130.4 2.0 fusion.212
  132.9 0.9 fusion.213
  133.8 0.9 fusion.214
  136.7 1.8 convolution_bitcast_fusion.4
  138.5 2.0 fusion.212
  141.9 0.9 fusion.214
  144.8 1.8 convolution_bitcast_fusion.4
  146.6 2.0 fusion.212
  150.0 0.9 fusion.214
  153.0 1.8 convolution_bitcast_fusion.4
  154.7 2.0 fusion.212
  158.1 0.9 fusion.214
  161.1 1.8 convolution_bitcast_fusion.4
  162.9 2.0 fusion.212
  165.3 0.9 fusion.213
  166.2 0.9 fusion.214
  169.2 1.8 convolution_bitcast_fusion.4
  171.0 2.0 fusion.212
  174.3 0.9 fusion.214
  177.3 1.8 convolution_bitcast_fusion.4
  179.1 2.0 fusion.212
  182.5 0.9 fusion.214
  184.1 42.6 %scatter_custom_fusion.2 = f32[9,131072]{0,1:T(8,128)} fusion(s32[1024]{0:T(1024)} %get-tuple-element.261, f32[]{:T(128)} %constant.125.clone.1, f32[1024,9]{1,0:T(8,128)S(1)} %copy.66, s32[1024]{0:T(1024)} %broadcast_clamp_fusion.1), kind=kCustom, calls=%fused_computation.125 | custom fusion | flops 9216 | bytes 4719104 | tf_op jit(solution)/shard_map/scatter-add | solution.py:256
  226.8 36.9 %copy.67 = f32[9,131072]{1,0:T(8,128)} copy(f32[9,131072]{0,1:T(8,128)} %scatter_custom_fusion.2) | data formatting | bytes 9437184 | tf_op jit(solution)/shard_map/scatter-add | solution.py:256
  263.8 147.5 %reduce-scatter.2.cloned.1.call-done = f32[9,2048]{1,0:T(8,128)} async-done(((f32[9,131072]{1,0:T(8,128)}), f32[9,2048]{1,0:T(8,128)}) %reduce-scatter.2.cloned.1.call-update) | async-done | bytes 73744 | tf_op jit(solution)/shard_map/reduce_scatter | solution.py:257
  411.3 0.9 split.5
  413.2 1.0 fusion.183
  415.9 1.1 multiply_multiply_fusion.2
  418.1 47.4 %all-reduce.23.cloned.1.call-done = f32[59,2048]{1,0:T(8,128)} async-done(((f32[59,2048]{1,0:T(8,128)}), f32[59,2048]{1,0:T(8,128)}) %all-reduce.23.cloned.1.call-update) | async-done | bytes 483344 | tf_op jit(solution)/shard_map/psum | solution.py:259
  465.5 2.4 divide_subtract_fusion
  (276 shorter events, 51.1 us)
Async XLA Ops:
  7.2 34.8 %copy-start = (f32[16,12]{1,0:T(8,128)S(1)}, f32[16,12]{1,0:T(8,128)}, u32[]{:S(2)}) copy-start(f32[16,12]{1,0:T(8,128)} %param.19) | copy-start | bytes 2308
  29.3 33.6 %all-to-all-start = ((s32[64,1,32]{2,1,0:T(1,128)}), s32[64,1,32]{2,1,0:T(1,128)S(1)}, u32[]{:S(2)}, u32[]{:S(2)}) async-start(s32[64,1,32]{2,1,0:T(1,128)} %bitcast.7), calls=%async_computation | async-start | bytes 65536 | tf_op jit(solution)/shard_map/all_to_all | solution.py:239
  45.2 3.1 copy-start.6
  69.9 19.7 %all-to-all-start.1 = ((f32[64,1,288]{2,1,0:T(1,128)}), f32[64,1,288]{2,1,0:T(1,128)S(1)}, u32[]{:S(2)}, u32[]{:S(2)}) async-start(f32[64,1,288]{2,1,0:T(1,128)} %reshape.822), calls=%async_computation.1 | async-start | bytes 196608 | tf_op jit(solution)/shard_map/all_to_all | solution.py:241
  80.2 331.1 %reduce-scatter.2.cloned.1.call-start = ((), (), s32[]{:S(2)}) async-start(), calls=%async_computation.3 | async-start | bytes 8519680 | tf_op jit(solution)/shard_map/reduce_scatter | solution.py:257
  184.0 231.6 %copy-start.1 = (f32[59,2048]{1,0:T(8,128)S(1)}, f32[59,2048]{1,0:T(8,128)}, u32[]{:S(2)}) copy-start(f32[59,2048]{1,0:T(8,128)} %param.15) | copy-start | bytes 1449988
  184.1 231.6 %copy-start.7 = (f32[3]{0:T(128)S(1)}, f32[3]{0:T(128)}, u32[]{:S(2)}) copy-start(f32[3]{0:T(128)} %copy-done.6) | copy-start | bytes 40
  184.1 231.7 %copy-start.4 = (f32[1,2048]{1,0:T(1,128)S(1)}, f32[1,2048]{1,0:T(1,128)}, u32[]{:S(2)}) copy-start(f32[1,2048]{1,0:T(1,128)} %get-tuple-element.381) | copy-start | bytes 24580
  184.1 231.7 %copy-start.5 = (f32[1,2048]{1,0:T(1,128)S(1)}, f32[1,2048]{1,0:T(1,128)}, u32[]{:S(2)}) copy-start(f32[1,2048]{1,0:T(1,128)} %get-tuple-element.382) | copy-start | bytes 24580
  184.1 281.4 %copy-start.2 = (f32[59,2048]{1,0:T(8,128)S(1)}, f32[59,2048]{1,0:T(8,128)}, u32[]{:S(2)}) copy-start(f32[59,2048]{1,0:T(8,128)} %param.16) | copy-start | bytes 1449988
  184.1 281.4 %copy-start.3 = (f32[59,2048]{1,0:T(8,128)S(1)}, f32[59,2048]{1,0:T(8,128)}, u32[]{:S(2)}) copy-start(f32[59,2048]{1,0:T(8,128)} %param.17) | copy-start | bytes 1449988
  184.1 281.4 %copy-start.8 = (f32[59]{0:T(128)S(1)}, f32[59]{0:T(128)}, u32[]{:S(2)}) copy-start(f32[59]{0:T(128)} %param.18) | copy-start | bytes 712
  263.7 201.8 %all-reduce.23.cloned.1.call-start = ((), (), s32[]{:S(2)}) async-start(), calls=%async_computation.4 | async-start | bytes 1048576 | tf_op jit(solution)/shard_map/psum | solution.py:259
Sparse Core Ops, SparseCore 0:
  263.9 147.4 reduce-scatter.1
  418.3 47.2 all-reduce.22
where the time goes:
time: 485 us; the launch traced here: 475 us
  waiting for transfers between devices  204 us (42%)
  other arithmetic  116 us (24%)
  local copies, waits for them, and re-layouts  74.5 us (15%)
  matrix products  40 us (8%)
  starting transfers between devices  22.4 us (5%)
  between operations  16.3 us (3%)
    reduce_scatter x1, waiting for transfers between devices, body(): lax.psum_scatter(dense, 'tiles', scatter_dimension=1, tiled=True)  148 us
    scatter-add x3, other arithmetic, body(): jnp.zeros((9, peers * owned), jnp.float32).at[:, global_ids].add(flat_grads)  47.6 us
    psum x1, waiting for transfers between devices, body(): total = lax.psum(param_grad, 'views')  47.4 us
    scatter-add x2, local copies, waits for them, and re-layouts, body(): jnp.zeros((9, peers * owned), jnp.float32).at[:, global_ids].add(flat_grads)  36.9 us
    dot_general x8, matrix products, backward(): lax.dot_general(resid, piece[6:9], (((0,), (0,)), ((), ())), precision=pr...  15.8 us
    dot_general x8, matrix products, backward(): color_grad = jnp.dot(resid, weight, precision=precise)  14.4 us
    all_to_all x1, starting transfers between devices, body(): lax.all_to_all(asked_for, 'tiles', split_axis=0, concat_axis=0, tiled=True)  12 us
    lt x16, other arithmetic, block_terms(): live = (start + jnp.arange(BLOCK) < count)[None, :]  10.5 us
  transfers between devices with their start and end apart: 4, of which 3 were waited for; matrix products, arithmetic and copies ran while one was open for 4% of the time, Pallas kernels for 0%

commit v1 on v0

--- a/solution.py
+++ b/solution.py
@@ -14,6 +14,16 @@
 decay_one = 0.9
 decay_two = 0.999
 adam_epsilon = 1e-08
+
+
+def _take_edges(inp):
+    full_n = lax.psum(1, "views")
+    z2 = inp
+    for src_i in [u for u in (1, 2, 4, 8, 16) if u < full_n]:
+        seen_now = tuple(((q, q ^ src_i) for q in range(full_n)))
+        n_now = lax.ppermute(z2, "views", seen_now)
+        z2 = z2 + n_now
+    return z2
 
 
 def sh_basis(direction):
@@ -256,7 +266,7 @@
     dense = jnp.zeros((9, peers * owned), jnp.float32).at[:, global_ids].add(flat_grads)
     attr_grad = lax.psum_scatter(dense, "tiles", scatter_dimension=1, tiled=True)
     param_grad = pullback(attr_grad)[0]
-    total = lax.psum(param_grad, "views")
+    total = _take_edges(param_grad)
     new_values, first_new, second_new = adam_step(
         gaussians, moment_one, moment_two, total, learn_rates
     )

time: 485 us -> 448 us (0.924)
  the two profiles are of different devices: /device:TPU:2 before, /device:TPU:24 now
where the time goes in v1:
time: 448 us; the launch traced here: 440 us
  waiting for transfers between devices  190 us (42%)
  other arithmetic  107 us (24%)
  local copies, waits for them, and re-layouts  75.9 us (17%)
  matrix products  25.2 us (6%)
  starting transfers between devices  23.3 us (5%)
  between operations  16.7 us (4%)
    reduce_scatter x1, waiting for transfers between devices, body(): lax.psum_scatter(dense, 'tiles', scatter_dimension=1, tiled=True)  157 us
    scatter-add x3, other arithmetic, body(): jnp.zeros((9, peers * owned), jnp.float32).at[:, global_ids].add(flat_grads)  46.2 us
    scatter-add x2, local copies, waits for them, and re-layouts, body(): jnp.zeros((9, peers * owned), jnp.float32).at[:, global_ids].add(flat_grads)  37.1 us
    ppermute x2, waiting for transfers between devices, _take_edges(): n_now = lax.ppermute(z2, 'views', seen_now)  22.8 us
    all_to_all x1, starting transfers between devices, body(): lax.all_to_all(asked_for, 'tiles', split_axis=0, concat_axis=0, tiled=True)  11.9 us
    all_to_all x1, waiting for transfers between devices, body(): lax.all_to_all(served, 'tiles', split_axis=1, concat_axis=1, tiled=True)  10.5 us
    all_to_all x1, starting transfers between devices, body(): lax.all_to_all(served, 'tiles', split_axis=1, concat_axis=1, tiled=True)  10.3 us
    lt x14, other arithmetic, block_terms(): live = (start + jnp.arange(BLOCK) < count)[None, :]  9.14 us
  transfers between devices with their start and end apart: 5, of which 4 were waited for; matrix products, arithmetic and copies ran while one was open for 4% of the time, Pallas kernels for 0%

profile of v1, /device:TPU:24, one launch (start us, length us, event | category | flops | bytes accessed | tf_op | source)
XLA Modules:
  0.0 439.6 jit_solution(12599499597651002821)
XLA Ops:
  7.2 5.1 %sort.17 = (s32[1024]{0:T(1024)}, s32[1024]{0:T(1024)S(1)}) sort(s32[1024]{0:T(1024)} %bitcast.355, s32[1024]{0:T(1024)S(1)} %iota.30), dimensions={0}, to_apply=%region_0.0 | sort | flops 10240 | bytes 16384 | tf_op jit(solution)/shard_map/jit(argsort)/sort | solution.py:235
  12.3 5.7 %gather_fusion = s32[1024]{0:T(1024)S(1)} fusion(s32[1024]{0:T(1024)} %bitcast.356, s32[1024]{0:T(1024)S(1)} %get-tuple-element.458), kind=kCustom, calls=%fused_computation | custom fusion | bytes 12288 | tf_op jit(solution)/shard_map/gather | solution.py:236
  18.0 5.7 %gather_fusion.1 = s32[1024]{0:T(1024)S(1)} fusion(s32[1024]{0:T(1024)} %bitcast.357, s32[1024]{0:T(1024)S(1)} %get-tuple-element.458), kind=kCustom, calls=%fused_computation.1 | custom fusion | bytes 12288 | tf_op jit(solution)/shard_map/gather | solution.py:246
  24.3 4.3 scatter_custom_fusion
  29.3 11.9 %all-to-all-start = ((s32[64,1,32]{2,1,0:T(1,128)}), s32[64,1,32]{2,1,0:T(1,128)S(1)}, u32[]{:S(2)}, u32[]{:S(2)}) async-start(s32[64,1,32]{2,1,0:T(1,128)} %bitcast.7), calls=%async_computation | async-start | bytes 65536 | tf_op jit(solution)/shard_map/all_to_all | solution.py:249
  42.7 0.9 multiply_reduce_fusion.9
  43.7 1.1 slice.164
  45.1 0.9 multiply_reduce_fusion.5
  46.1 1.0 convolution_add_fusion.2
  47.2 1.0 broadcast_divide_fusion
  48.2 1.1 broadcast_multiply_fusion.10
  50.0 0.9 subtract_multiply_fusion.21
  53.7 3.8 sort.18
  58.8 4.3 scatter_custom_fusion.1
  63.2 5.5 %gather_fusion.2 = f32[2048,9]{1,0:T(8,128)S(1)} fusion(f32[9,2048]{0,1:T(8,128)S(1)} %copy.61, s32[2048]{0:T(1024)S(1)} %broadcast_clamp_fusion), kind=kCustom, calls=%fused_computation.2 | custom fusion | bytes 155648 | tf_op jit(solution)/shard_map/jit(_take)/gather | solution.py:250
  70.1 10.3 %all-to-all-start.1 = ((f32[64,1,288]{2,1,0:T(1,128)}), f32[64,1,288]{2,1,0:T(1,128)S(1)}, u32[]{:S(2)}, u32[]{:S(2)}) async-start(f32[64,1,288]{2,1,0:T(1,128)} %reshape.822), calls=%async_computation.1 | async-start | bytes 196608 | tf_op jit(solution)/shard_map/all_to_all | solution.py:251
  80.5 10.5 %all-to-all-done.1 = f32[64,1,288]{2,1,0:T(1,128)S(1)} async-done(((f32[64,1,288]{2,1,0:T(1,128)}), f32[64,1,288]{2,1,0:T(1,128)S(1)}, u32[]{:S(2)}, u32[]{:S(2)}) %all-to-all-start.1) | async-done | bytes 73760 | tf_op jit(solution)/shard_map/all_to_all | solution.py:251
  92.9 2.8 gather_fusion.3
  96.0 19.9 %while.40 = (s32[]{:T(128)}, f32[3,1024]{1,0:T(4,128)S(1)}, f32[1024]{0:T(1024)S(1)}, s32[]{:T(128)}, f32[9,1024]{1,0:T(8,128)S(1)}, /*index=5*/s32[]{:T(128)}, ...) while((s32[]{:T(128)}, f32[3,1024]{1,0:T(4,128)S(1)}, ...), condition=%wide.region_15.16_spmd.clone, body=%wide.region_12.15_spmd.clone.sunk | while | flops 25580940 | bytes 2186327 | solution.py:156
  98.2 1.0 convolution_add_fusion.4
  101.0 1.0 convolution_add_fusion.4
  103.8 1.0 convolution_add_fusion.4
  106.6 1.0 convolution_add_fusion.4
  109.3 1.0 convolution_add_fusion.4
  112.1 1.0 convolution_add_fusion.4
  114.9 1.0 convolution_add_fusion.4
  115.9 1.4 multiply_reduce_fusion.10
  117.3 46.9 %while.41 = (s32[]{:T(128)}, f32[9,1024]{1,0:T(8,128)S(1)}, f32[1024]{0:T(1024)S(1)}, f32[1024]{0:T(1024)S(1)}, s32[]{:T(128)}, /*index=5*/f32[9,1024]{1,0:T(8,1...) while((s32[]{:T(128)}, f32[9,1024]{1,0:T(8,128)S(1)}, ...), condition=%wide.region_27.28_spmd.clone, body=%wide.region_17.27_spmd.clone.sunk | while | flops 55855884 | bytes 9098243 | solution.py:194
  119.1 1.1 convolution_bitcast_fusion.4
  120.2 1.3 fusion.213
  121.9 0.9 fusion.214
  122.8 0.9 fusion.215
  125.8 1.1 convolution_bitcast_fusion.4
  126.9 1.3 fusion.213
  128.6 0.9 fusion.214
  129.5 0.9 fusion.215
  132.5 1.1 convolution_bitcast_fusion.4
  133.6 1.3 fusion.213
  135.3 0.9 fusion.214
  136.2 0.9 fusion.215
  139.2 1.1 convolution_bitcast_fusion.4
  140.3 1.3 fusion.213
  142.0 0.9 fusion.214
  142.9 0.9 fusion.215
  145.9 1.1 convolution_bitcast_fusion.4
  147.0 1.2 fusion.213
  148.7 0.9 fusion.214
  149.6 0.9 fusion.215
  152.6 1.1 convolution_bitcast_fusion.4
  153.6 1.3 fusion.213
  156.3 0.9 fusion.215
  159.3 1.1 convolution_bitcast_fusion.4
  160.3 1.3 fusion.213
  163.0 0.9 fusion.215
  164.6 42.5 %scatter_custom_fusion.2 = f32[9,131072]{0,1:T(8,128)} fusion(s32[1024]{0:T(1024)S(1)} %get-tuple-element.261, f32[]{:T(128)} %constant.125.clone.1, f32[1024,9]{1,0:T(8,128)S(1)} %copy.66, s32[1024]{0:T(1024)S(1)} %broadcast_clamp_fusion.1), kind=kCustom, calls=%fused_computation.125 | custom fusion | flops 9216 | bytes 4718596 | tf_op jit(solution)/shard_map/scatter-add | solution.py:266
  207.1 37.1 %copy.67 = f32[9,131072]{1,0:T(8,128)} copy(f32[9,131072]{0,1:T(8,128)} %scatter_custom_fusion.2) | data formatting | bytes 9437184 | tf_op jit(solution)/shard_map/scatter-add | solution.py:266
  244.3 156.7 %reduce-scatter.2.cloned.1.call-done = f32[9,2048]{1,0:T(8,128)} async-done(((f32[9,131072]{1,0:T(8,128)}), f32[9,2048]{1,0:T(8,128)}) %reduce-scatter.2.cloned.1.call-update) | async-done | bytes 73744 | tf_op jit(solution)/shard_map/reduce_scatter | solution.py:267
  401.0 0.9 split.5
  402.8 1.0 fusion.184
  405.7 1.1 multiply_multiply_fusion.2
  407.1 1.0 collective-permute-start
  408.1 12.2 %collective-permute-done = f32[59,2048]{1,0:T(8,128)S(1)} collective-permute-done((f32[59,2048]{1,0:T(8,128)S(1)}, f32[59,2048]{1,0:T(8,128)S(1)}, u32[]{:S(2)}, u32[]{:S(2)}) %collective-permute-start) | collective-permute-done | bytes 483360 | tf_op jit(solution)/shard_map/ppermute | solution.py:24
  420.4 10.7 %collective-permute-done.1 = f32[59,2048]{1,0:T(8,128)S(1)} collective-permute-done((f32[59,2048]{1,0:T(8,128)S(1)}, f32[59,2048]{1,0:T(8,128)S(1)}, u32[]{:S(2)}, u32[]{:S(2)}) %collective-permute-start.1) | collective-permute-done | bytes 483360 | tf_op jit(solution)/shard_map/ppermute | solution.py:24
  431.1 1.4 divide_subtract_fusion
  (309 shorter events, 45.0 us)
Async XLA Ops:
  7.2 34.7 %copy-start = (f32[16,12]{1,0:T(8,128)S(1)}, f32[16,12]{1,0:T(8,128)}, u32[]{:S(2)}) copy-start(f32[16,12]{1,0:T(8,128)} %param.19) | copy-start | bytes 2308
  29.3 33.8 %all-to-all-start = ((s32[64,1,32]{2,1,0:T(1,128)}), s32[64,1,32]{2,1,0:T(1,128)S(1)}, u32[]{:S(2)}, u32[]{:S(2)}) async-start(s32[64,1,32]{2,1,0:T(1,128)} %bitcast.7), calls=%async_computation | async-start | bytes 65536 | tf_op jit(solution)/shard_map/all_to_all | solution.py:249
  46.1 5.1 %copy-start.4 = (f32[2048]{0:T(1024)}, f32[2048]{0:T(1024)S(1)}, u32[]{:S(2)}) copy-start(f32[2048]{0:T(1024)S(1)} %sqrt.40) | copy-start | bytes 24580
  47.1 4.0 copy-start.10
  47.2 6.3 %copy-start.26 = (f32[1,2048]{1,0:T(1,128)}, f32[1,2048]{1,0:T(1,128)S(1)}, u32[]{:S(2)}) copy-start(f32[1,2048]{1,0:T(1,128)S(1)} %get-tuple-element.454) | copy-start | bytes 24580
  47.2 6.3 %copy-start.28 = (f32[1,2048]{1,0:T(1,128)}, f32[1,2048]{1,0:T(1,128)S(1)}, u32[]{:S(2)}) copy-start(f32[1,2048]{1,0:T(1,128)S(1)} %get-tuple-element.412) | copy-start | bytes 24580
  49.3 1.9 copy-start.6
  49.3 1.9 copy-start.8
  49.4 0.6 copy-start.22
  50.9 0.6 copy-start.18
  50.9 0.6 copy-start.20
  52.0 65.3 %copy-start.12 = (f32[1,3,2048]{2,0,1:T(1,128)}, f32[1,3,2048]{2,0,1:T(1,128)S(1)}, u32[]{:S(2)}) copy-start(f32[1,3,2048]{2,0,1:T(1,128)S(1)} %get-tuple-element.406) | copy-start | bytes 73732
  52.0 65.3 %copy-start.14 = (f32[1,3,2048]{2,0,1:T(1,128)}, f32[1,3,2048]{2,0,1:T(1,128)S(1)}, u32[]{:S(2)}) copy-start(f32[1,3,2048]{2,0,1:T(1,128)S(1)} %get-tuple-element.407) | copy-start | bytes 73732
  52.0 65.3 %copy-start.16 = (f32[1,3,2048]{2,0,1:T(1,128)}, f32[1,3,2048]{2,0,1:T(1,128)S(1)}, u32[]{:S(2)}) copy-start(f32[1,3,2048]{2,0,1:T(1,128)S(1)} %get-tuple-element.408) | copy-start | bytes 73732
  52.7 0.6 copy-start.34
  52.7 0.8 copy-start.30
  52.7 0.8 copy-start.32
  70.1 20.8 %all-to-all-start.1 = ((f32[64,1,288]{2,1,0:T(1,128)}), f32[64,1,288]{2,1,0:T(1,128)S(1)}, u32[]{:S(2)}, u32[]{:S(2)}) async-start(f32[64,1,288]{2,1,0:T(1,128)} %reshape.822), calls=%async_computation.1 | async-start | bytes 196608 | tf_op jit(solution)/shard_map/all_to_all | solution.py:251
  80.4 320.5 %reduce-scatter.2.cloned.1.call-start = ((), (), s32[]{:S(2)}) async-start(), calls=%async_computation.3 | async-start | bytes 8519680 | tf_op jit(solution)/shard_map/reduce_scatter | solution.py:267
  164.4 237.9 %copy-start.23 = (f32[1,2048]{1,0:T(1,128)S(1)}, f32[1,2048]{1,0:T(1,128)}, u32[]{:S(2)}) copy-start(f32[1,2048]{1,0:T(1,128)} %copy-done.22) | copy-start | bytes 24580
  164.4 239.4 %copy-start.31 = (f32[2048]{0:T(1024)S(1)}, f32[2048]{0:T(1024)}, u32[]{:S(2)}) copy-start(f32[2048]{0:T(1024)} %copy-done.30) | copy-start | bytes 24580
  164.4 239.4 %copy-start.33 = (f32[2048]{0:T(1024)S(1)}, f32[2048]{0:T(1024)}, u32[]{:S(2)}) copy-start(f32[2048]{0:T(1024)} %copy-done.32) | copy-start | bytes 24580
  164.4 239.4 %copy-start.35 = (f32[2048]{0:T(1024)S(1)}, f32[2048]{0:T(1024)}, u32[]{:S(2)}) copy-start(f32[2048]{0:T(1024)} %copy-done.34) | copy-start | bytes 24580
  164.4 239.4 %copy-start.27 = (f32[1,2048]{1,0:T(1,128)S(1)}, f32[1,2048]{1,0:T(1,128)}, u32[]{:S(2)}) copy-start(f32[1,2048]{1,0:T(1,128)} %copy-done.26) | copy-start | bytes 24580
  164.5 239.4 %copy-start.29 = (f32[1,2048]{1,0:T(1,128)S(1)}, f32[1,2048]{1,0:T(1,128)}, u32[]{:S(2)}) copy-start(f32[1,2048]{1,0:T(1,128)} %copy-done.28) | copy-start | bytes 24580
  164.5 240.1 %copy-start.5 = (f32[2048]{0:T(1024)S(1)}, f32[2048]{0:T(1024)}, u32[]{:S(2)}) copy-start(f32[2048]{0:T(1024)} %copy-done.4) | copy-start | bytes 24580
  164.5 240.1 %copy-start.7 = (f32[1,2048]{1,0:T(1,128)S(1)}, f32[1,2048]{1,0:T(1,128)}, u32[]{:S(2)}) copy-start(f32[1,2048]{1,0:T(1,128)} %copy-done.6) | copy-start | bytes 24580
  164.5 240.1 %copy-start.9 = (f32[1,2048]{1,0:T(1,128)S(1)}, f32[1,2048]{1,0:T(1,128)}, u32[]{:S(2)}) copy-start(f32[1,2048]{1,0:T(1,128)} %copy-done.8) | copy-start | bytes 24580
  164.5 240.1 %copy-start.19 = (f32[1,2048]{1,0:T(1,128)S(1)}, f32[1,2048]{1,0:T(1,128)}, u32[]{:S(2)}) copy-start(f32[1,2048]{1,0:T(1,128)} %copy-done.18) | copy-start | bytes 24580
  164.5 240.1 %copy-start.21 = (f32[1,2048]{1,0:T(1,128)S(1)}, f32[1,2048]{1,0:T(1,128)}, u32[]{:S(2)}) copy-start(f32[1,2048]{1,0:T(1,128)} %copy-done.20) | copy-start | bytes 24580
  164.5 240.5 %copy-start.13 = (f32[1,3,2048]{2,0,1:T(1,128)S(1)}, f32[1,3,2048]{2,0,1:T(1,128)}, u32[]{:S(2)}) copy-start(f32[1,3,2048]{2,0,1:T(1,128)} %copy-done.12) | copy-start | bytes 73732
  164.5 240.5 %copy-start.15 = (f32[1,3,2048]{2,0,1:T(1,128)S(1)}, f32[1,3,2048]{2,0,1:T(1,128)}, u32[]{:S(2)}) copy-start(f32[1,3,2048]{2,0,1:T(1,128)} %copy-done.14) | copy-start | bytes 73732
  164.5 240.5 %copy-start.17 = (f32[1,3,2048]{2,0,1:T(1,128)S(1)}, f32[1,3,2048]{2,0,1:T(1,128)}, u32[]{:S(2)}) copy-start(f32[1,3,2048]{2,0,1:T(1,128)} %copy-done.16) | copy-start | bytes 73732
  164.5 240.5 %copy-start.24 = (f32[3,2048]{1,0:T(4,128)S(1)}, f32[3,2048]{1,0:T(4,128)}, u32[]{:S(2)}) copy-start(f32[3,2048]{1,0:T(4,128)} %get-tuple-element.338) | copy-start | bytes 73732
  164.6 240.5 %copy-start.25 = (f32[3,2048]{1,0:T(4,128)S(1)}, f32[3,2048]{1,0:T(4,128)}, u32[]{:S(2)}) copy-start(f32[3,2048]{1,0:T(4,128)} %get-tuple-element.339) | copy-start | bytes 73732
  164.6 240.9 %copy-start.1 = (f32[59,2048]{1,0:T(8,128)S(1)}, f32[59,2048]{1,0:T(8,128)}, u32[]{:S(2)}) copy-start(f32[59,2048]{1,0:T(8,128)} %param.15) | copy-start | bytes 1449988
  164.6 241.1 %copy-start.11 = (f32[3,2048]{1,0:T(4,128)S(1)}, f32[3,2048]{1,0:T(4,128)}, u32[]{:S(2)}) copy-start(f32[3,2048]{1,0:T(4,128)} %copy-done.10) | copy-start | bytes 73732
  164.6 266.5 %copy-start.2 = (f32[59,2048]{1,0:T(8,128)S(1)}, f32[59,2048]{1,0:T(8,128)}, u32[]{:S(2)}) copy-start(f32[59,2048]{1,0:T(8,128)} %param.16) | copy-start | bytes 1449988
  164.6 266.5 %copy-start.3 = (f32[59,2048]{1,0:T(8,128)S(1)}, f32[59,2048]{1,0:T(8,128)}, u32[]{:S(2)}) copy-start(f32[59,2048]{1,0:T(8,128)} %param.17) | copy-start | bytes 1449988
  164.6 266.5 %copy-start.36 = (f32[59]{0:T(128)S(1)}, f32[59]{0:T(128)}, u32[]{:S(2)}) copy-start(f32[59]{0:T(128)} %param.18) | copy-start | bytes 712
  407.1 13.1 %collective-permute-start = (f32[59,2048]{1,0:T(8,128)S(1)}, f32[59,2048]{1,0:T(8,128)S(1)}, u32[]{:S(2)}, u32[]{:S(2)}) collective-permute-start(f32[59,2048]{1,0:T(8,128)S(1)} %pad_add_fusion), channel_id=1, source_target_pairs={{0,1},{1,0},{2,3},{3,2},{4,5},{5,4},{6,7},{7,6},{8,9},{9,8},{10,11... | collective-permute-start | bytes 1449992 | tf_op jit(solution)/shard_map/ppermute | solution.py:24
  420.3 10.8 %collective-permute-start.1 = (f32[59,2048]{1,0:T(8,128)S(1)}, f32[59,2048]{1,0:T(8,128)S(1)}, u32[]{:S(2)}, u32[]{:S(2)}) collective-permute-start(f32[59,2048]{1,0:T(8,128)S(1)} %fusion.180), channel_id=1, source_target_pairs={{0,2},{1,3},{2,0},{3,1},{4,6},{5,7},{6,4},{7,5},{8,10},{9,11},{10,... | collective-permute-start | bytes 1449992 | tf_op jit(solution)/shard_map/ppermute | solution.py:24
Sparse Core Ops, SparseCore 0:
  244.4 156.5 reduce-scatter.1
